TPU v7x, 256 devices: a whole 4x4x8 slice. The times are simulated.
256 devices in a mesh: mem: 4 (over x), col: 64 (over y, z, core).
Axes of the slice: x: 4, y: 4, z: 8, core: 2. Of those that a mesh axis runs over, the one named last changes fastest.
Arguments:
- perturbations: bfloat16 [32, 256, 256, 128], P('mem', 'col'), may hold values from -4 to 4
- static_root: float32 [128, 128], replicated, may hold values from -0.5 to 1.5
- obs_jacobian: float32 [128, 128], replicated, may hold values from -0.5 to 0.5
- innovations: float32 [16384, 128], P('col'), may hold values from -6 to 6
- obs_weights: float32 [128], replicated, may hold values from 0.2 to 2
- length_scale: float32 [256, 256], P('col'), may hold values from 0.05 to 0.24
- obs_owner: int32 [16384, 1], P('col'), may hold values from 0 to 63; in each aligned block of 256 rows (0 to 255, 256 to 511, ...) at most 8 rows name the same one
- obs_cell: int32 [16384], P('col'), may hold values from 0 to 1023
- obs_count: int32 [64], P('col'), may hold values from 128 to 256, as said below
Outputs:
- increment: float32 [256, 256, 128], P('col', 'mem')
- control_static: float32 [256, 256, 128], P('col', 'mem')
- control_ensemble: float32 [32, 256, 256], P('mem', 'col')
Inputs may be any that keep to these rules, and one draw needn't show every extreme that they name: `obs_owner`: each holder's 256 rows name any one column block at most 8 times. `obs_count`: rows at or past a holder's count are padding and are ignored; at least one holder is full. `obs_cell`: the column within the owner's block, numbered y * 256 + x, where y is its grid row within the block (0 to 3).
All inputs are finite; a program needn't handle non-finite values.
Results may differ from a plain program's by a relative error of at most 0.004.
Values may be sent and summed in bfloat16 or wider, within the bound.
No kernel may reach another device: no remote copies, remote signals or barrier semaphores. Data moves between devices by JAX's collectives and lax.ppermute only.
A program may use at most 64 MiB of HBM per device.

v0:
```python
import jax
import jax.numpy as jnp
from jax import lax
from jax.sharding import PartitionSpec as P

NSWEEP = 4
ITERS = 2


def extended(block, sides, width):
    for axis, dim in sides:
        count = lax.axis_size(axis)
        forward = [(i, i + 1) for i in range(count - 1)]
        backward = [(target, source) for source, target in forward]
        low = lax.ppermute(
            lax.slice_in_dim(block, block.shape[dim] - width, None, axis=dim), axis, forward
        )
        high = lax.ppermute(lax.slice_in_dim(block, 0, width, axis=dim), axis, backward)
        block = jnp.concatenate([low, block, high], axis=dim)
    return block


def face_coefficients(length_scale):
    rimmed = extended(length_scale, (("col", 0),), 1)
    padded = jnp.pad(rimmed, ((0, 0), (1, 1)))
    return (
        jnp.sqrt(length_scale * padded[:-2, 1:-1]),
        jnp.sqrt(length_scale * padded[2:, 1:-1]),
        jnp.sqrt(length_scale * padded[1:-1, :-2]),
        jnp.sqrt(length_scale * padded[1:-1, 2:]),
    )


def sweeps(values, coeffs):
    face_up, face_down, face_left, face_right = coeffs
    for sweep_step in range(NSWEEP):
        rimmed = extended(values, (("col", 1),), 1)
        padded = jnp.pad(rimmed, ((0, 0), (0, 0), (1, 1)))
        centre = values
        values = (
            centre
            + face_up * (padded[:, :-2, 1:-1] - centre)
            + face_down * (padded[:, 2:, 1:-1] - centre)
            + face_left * (padded[:, 1:-1, :-2] - centre)
            + face_right * (padded[:, 1:-1, 2:] - centre)
        )
    return values


def local_inner(first, second):
    return jnp.sum(first[0] * second[0]) + jnp.sum(first[1] * second[1])


def shards(
    perturbations,
    static_root,
    obs_jacobian,
    innovations,
    obs_weights,
    length_scale,
    obs_owner,
    obs_cell,
    obs_count,
):
    members, rows_here, columns, features = perturbations.shape
    quarter = columns // lax.axis_size("mem")
    offset = lax.axis_index("mem") * quarter
    blocks = lax.axis_size("col")
    obs_dev, channels = innovations.shape
    capacity = max(2, 2 * obs_dev // blocks)
    total_slots = blocks * capacity
    coeffs = face_coefficients(length_scale)
    is_live = jnp.arange(obs_dev, dtype=jnp.int32) < obs_count[0]
    owner_ids = obs_owner[:, 0]
    onehot = (
        (owner_ids[:, None] == jnp.arange(blocks, dtype=jnp.int32)[None, :]) & is_live[:, None]
    ).astype(jnp.int32)
    slot_rank = jnp.sum((jnp.cumsum(onehot, axis=0) - onehot) * onehot, axis=1)
    slot_ids = jnp.where(is_live, owner_ids * capacity + slot_rank, total_slots)
    send_values = (
        jnp.zeros((total_slots, channels), jnp.float32).at[slot_ids].set(innovations, mode="drop")
    )
    send_cells = jnp.zeros((total_slots,), jnp.int32).at[slot_ids].set(obs_cell, mode="drop")
    send_marks = jnp.zeros((total_slots,), jnp.float32).at[slot_ids].set(1.0, mode="drop")
    got_values, got_cells, got_marks = (
        lax.all_to_all(
            send_values.reshape(blocks, capacity, channels),
            "col",
            split_axis=0,
            concat_axis=0,
            tiled=True,
        ),
        lax.all_to_all(
            send_cells.reshape(blocks, capacity), "col", split_axis=0, concat_axis=0, tiled=True
        ),
        lax.all_to_all(
            send_marks.reshape(blocks, capacity), "col", split_axis=0, concat_axis=0, tiled=True
        ),
    )
    got_values = got_values.reshape(total_slots, channels)
    got_cells = got_cells.reshape(total_slots)
    got_marks = got_marks.reshape(total_slots)
    obs_index = got_cells
    obs_gain = got_marks[:, None] * obs_weights[None, :]

    def spread_back(weighted):
        back = jnp.dot(weighted, obs_jacobian.T, precision=lax.Precision.HIGHEST)
        grid = jnp.zeros((rows_here * columns, features), jnp.float32).at[obs_index].add(back)
        return grid.reshape(rows_here, columns, features)

    def adjoint_map(gradient):
        own_gradient = lax.dynamic_slice_in_dim(gradient, offset, quarter, 1)
        rounded = gradient.astype(jnp.bfloat16)
        static = jnp.dot(
            own_gradient.reshape(rows_here * quarter, features),
            static_root.T,
            precision=lax.Precision.HIGHEST,
        ).reshape(rows_here, quarter, features)
        projected = jnp.einsum(
            "kyxf,yxf->kyx", perturbations, rounded, preferred_element_type=jnp.float32
        )
        return (static, sweeps(projected, coeffs))

    residual = adjoint_map(spread_back(obs_gain * got_values))
    direction = residual
    state = (jnp.zeros_like(residual[0]), jnp.zeros_like(residual[1]))
    increment = jnp.zeros((rows_here, quarter, features), jnp.float32)
    norm_now = lax.psum(local_inner(residual, residual), ("mem", "col"))
    for iteration in range(ITERS):
        smoothed = sweeps(direction[1], coeffs).astype(jnp.bfloat16)
        partial_sum = jnp.einsum(
            "kyxf,kyx->yxf", perturbations, smoothed, preferred_element_type=jnp.float32
        )
        forward_static = jnp.dot(
            direction[0].reshape(rows_here * quarter, features),
            static_root,
            precision=lax.Precision.HIGHEST,
        ).reshape(rows_here, quarter, features)
        own_slice = lax.dynamic_slice_in_dim(partial_sum, offset, quarter, 1) + forward_static
        partial_sum = lax.dynamic_update_slice_in_dim(partial_sum, own_slice, offset, 1)
        image_part = lax.psum(partial_sum, "mem")
        own_image = lax.dynamic_slice_in_dim(image_part, offset, quarter, 1)
        image_part, own_image = (image_part, own_image)
        gathered = image_part.reshape(rows_here * columns, features)[obs_index]
        model_obs = jnp.dot(gathered, obs_jacobian, precision=lax.Precision.HIGHEST)
        adj_static, adj_ensemble = adjoint_map(spread_back(obs_gain * model_obs))
        image = (direction[0] + adj_static, direction[1] + adj_ensemble)
        step = norm_now / lax.psum(local_inner(direction, image), ("mem", "col"))
        residual = (residual[0] - step * image[0], residual[1] - step * image[1])
        norm_next = lax.psum(local_inner(residual, residual), ("mem", "col"))
        state = (state[0] + step * direction[0], state[1] + step * direction[1])
        increment = increment + step * own_image
        ratio = norm_next / norm_now
        direction = (residual[0] + ratio * direction[0], residual[1] + ratio * direction[1])
        norm_now = norm_next
    return (increment, state[0], state[1])


def solution(mesh):
    placed = (
        P("mem", "col", None, None),
        P(),
        P(),
        P("col", None),
        P(),
        P("col", None),
        P("col", None),
        P("col"),
        P("col"),
    )
    return jax.shard_map(
        shards,
        mesh=mesh,
        in_specs=placed,
        out_specs=(P("col", "mem", None), P("col", "mem", None), P("mem", "col", None)),
        check_vma=False,
    )
```

profile of v0, /device:TPU:1, one launch (start us, length us, event | category | flops | bytes accessed | tf_op | source)
XLA Modules:
  0.0 626.9 jit_solution(7078985824332760388)
XLA Ops:
  13.3 13.1 %all-to-all-start = ((s32[64,1,8]{2,1,0:T(1,128)}), s32[64,1,8]{2,1,0:T(1,128)S(1)}, u32[]{:S(2)}, u32[]{:S(2)}) async-start(s32[64,1,8]{2,1,0:T(1,128)} %bitcast.6), calls=%async_computation | async-start | bytes 65536 | tf_op jit(solution)/shard_map/all_to_all | solution.py:93
  28.5 7.1 %all-to-all-done = s32[64,1,8]{2,1,0:T(1,128)S(1)} async-done(((s32[64,1,8]{2,1,0:T(1,128)}), s32[64,1,8]{2,1,0:T(1,128)S(1)}, u32[]{:S(2)}, u32[]{:S(2)}) %all-to-all-start) | async-done | bytes 2080 | tf_op jit(solution)/shard_map/all_to_all | solution.py:93
  35.7 4.7 all-to-all-start.1
  42.5 7.2 %all-to-all-done.1 = f32[64,1,8]{2,1,0:T(1,128)S(1)} async-done(((f32[64,1,8]{2,1,0:T(1,128)}), f32[64,1,8]{2,1,0:T(1,128)S(1)}, u32[]{:S(2)}, u32[]{:S(2)}) %all-to-all-start.1) | async-done | bytes 2080 | tf_op jit(solution)/shard_map/all_to_all | solution.py:96
  49.7 4.7 all-to-all-start.2
  55.3 3.5 collective-permute-start
  60.7 3.2 collective-permute-done.2
  68.7 2.4 scatter_custom_fusion.3
  73.1 3.3 collective-permute-start.1
  78.4 2.9 collective-permute-done.3
  86.0 2.6 collective-permute-done.5
  93.2 2.9 collective-permute-done.7
  98.3 2.4 collective-permute-start.9
  100.7 4.8 collective-permute-done.9
  107.9 2.4 collective-permute-start.11
  110.3 3.8 collective-permute-done.11
  118.7 3.8 collective-permute-done.13
  124.7 2.4 collective-permute-start.15
  128.0 2.9 collective-permute-done.15
  133.1 2.4 collective-permute-start.17
  136.4 2.9 collective-permute-done.17
  142.6 54.8 %all-reduce.25.cloned.1.call-done = f32[4,256,128]{2,1,0:T(8,128)} async-done(((f32[4,256,128]{2,1,0:T(8,128)}), f32[4,256,128]{2,1,0:T(8,128)}) %all-reduce.25.cloned.1.call-update) | async-done | bytes 524304 | tf_op jit(solution)/shard_map/psum | solution.py:141
  200.2 2.4 scatter_custom_fusion.4
  202.7 2.4 fusion.6
  206.3 6.9 %collective-permute-start.18 = (f32[8,1,256]{2,1,0:T(1,128)S(1)}, f32[8,1,256]{2,1,0:T(1,128)S(1)}, u32[]{:S(2)}, u32[]{:S(2)}) collective-permute-start(f32[8,1,256]{2,1,0:T(1,128)S(1)} %get-tuple-element.30), channel_id=1, source_target_pairs={{0,1},{1,2},{2,3},{3,4},{4,5},{5,6},{6,7},{7,8},{8,9},{9,10},{10,1... | collective-permute-start | bytes 24584 | tf_op jit(solution)/shard_map/ppermute | solution.py:15
  215.1 3.0 collective-permute-done.19
  220.4 2.4 collective-permute-start.21
  222.8 2.6 collective-permute-done.21
  227.6 2.4 collective-permute-start.23
  230.0 2.6 collective-permute-done.23
  238.0 3.9 collective-permute-done.25
  245.4 80.6 %all-reduce.21 = (f32[]{:T(128)}, f32[]{:T(128)}) all-reduce(f32[]{:T(128)S(6)} %add.401, f32[]{:T(128)S(6)} %add.437), channel_id=1, replica_groups=mesh['mem'=4,'col'=64] {'mem','col'}, use_global_device_ids=true, to_apply=%region_9.10 | all-reduce | flops 2 | bytes 16 | tf_op jit(solution)/shard_map/psum | solution.py:128
  329.9 73.2 %psum.45 = f32[]{:T(128)} all-reduce(f32[]{:T(128)S(6)} %add.438), channel_id=1, replica_groups=mesh['mem'=4,'col'=64] {'mem','col'}, use_global_device_ids=true, to_apply=%region_17.18 | all-reduce | flops 1 | bytes 8 | tf_op jit(solution)/shard_map/psum | solution.py:150
  404.4 4.2 collective-permute-start.26
  410.8 2.8 collective-permute-done.27
  418.3 2.6 collective-permute-done.29
  425.5 2.6 collective-permute-done.31
  432.7 2.6 collective-permute-done.33
  436.6 2.8 fusion.4
  440.4 48.7 %all-reduce.27.cloned.1.call-done = f32[4,256,128]{2,1,0:T(8,128)} async-done(((f32[4,256,128]{2,1,0:T(8,128)}), f32[4,256,128]{2,1,0:T(8,128)}) %all-reduce.27.cloned.1.call-update) | async-done | bytes 524304 | tf_op jit(solution)/shard_map/psum | solution.py:141
  492.0 2.4 scatter_custom_fusion.5
  494.5 2.4 fusion.2
  498.1 6.8 %collective-permute-start.34 = (f32[8,1,256]{2,1,0:T(1,128)S(1)}, f32[8,1,256]{2,1,0:T(1,128)S(1)}, u32[]{:S(2)}, u32[]{:S(2)}) collective-permute-start(f32[8,1,256]{2,1,0:T(1,128)S(1)} %get-tuple-element.14), channel_id=1, source_target_pairs={{0,1},{1,2},{2,3},{3,4},{4,5},{5,6},{6,7},{7,8},{8,9},{9,10},{10,1... | collective-permute-start | bytes 24584 | tf_op jit(solution)/shard_map/ppermute | solution.py:15
  506.9 3.0 collective-permute-done.35
  514.5 2.6 collective-permute-done.37
  521.7 2.6 collective-permute-done.39
  529.8 4.0 collective-permute-done.41
  535.9 80.6 %psum.47 = f32[]{:T(128)} all-reduce(f32[]{:T(128)S(6)} %add.476), channel_id=1, replica_groups=mesh['mem'=4,'col'=64] {'mem','col'}, use_global_device_ids=true, to_apply=%region_22.23 | all-reduce | flops 1 | bytes 8 | tf_op jit(solution)/shard_map/psum | solution.py:148
  (188 shorter events, 108.7 us)
Async XLA Ops:
  7.2 64.0 %copy-start = (bf16[8,4,256,128]{3,2,1,0:T(8,128)(2,1)S(1)}, bf16[8,4,256,128]{3,2,1,0:T(8,128)(2,1)}, u32[]{:S(2)}) copy-start(bf16[8,4,256,128]{3,2,1,0:T(8,128)(2,1)} %param.9) | copy-start | bytes 6291460
  13.3 22.4 %all-to-all-start = ((s32[64,1,8]{2,1,0:T(1,128)}), s32[64,1,8]{2,1,0:T(1,128)S(1)}, u32[]{:S(2)}, u32[]{:S(2)}) async-start(s32[64,1,8]{2,1,0:T(1,128)} %bitcast.6), calls=%async_computation | async-start | bytes 65536 | tf_op jit(solution)/shard_map/all_to_all | solution.py:93
  35.7 14.1 %all-to-all-start.1 = ((f32[64,1,8]{2,1,0:T(1,128)}), f32[64,1,8]{2,1,0:T(1,128)S(1)}, u32[]{:S(2)}, u32[]{:S(2)}) async-start(f32[64,1,8]{2,1,0:T(1,128)} %bitcast.8), calls=%async_computation.1 | async-start | bytes 65536 | tf_op jit(solution)/shard_map/all_to_all | solution.py:96
  49.7 17.7 %all-to-all-start.2 = ((f32[64,8,128]{2,1,0:T(8,128)}), f32[64,8,128]{2,1,0:T(8,128)S(1)}, u32[]{:S(2)}, u32[]{:S(2)}) async-start(f32[64,8,128]{2,1,0:T(8,128)} %bitcast.9), calls=%async_computation.2 | async-start | bytes 524288 | tf_op jit(solution)/shard_map/all_to_all | solution.py:86
  54.4 142.9 %all-reduce.25.cloned.1.call-start = ((), (), s32[]{:S(2)}) async-start(), calls=%async_computation.3 | async-start | bytes 1048576 | tf_op jit(solution)/shard_map/psum | solution.py:141
  55.3 5.5 collective-permute-start
  58.8 5.2 collective-permute-start.2
  73.1 5.3 collective-permute-start.1
  76.4 5.0 collective-permute-start.3
  81.6 4.3 collective-permute-start.4
  83.6 5.0 collective-permute-start.5
  88.8 4.3 collective-permute-start.6
  90.8 5.2 collective-permute-start.7
  96.3 4.3 collective-permute-start.8
  98.3 7.2 %collective-permute-start.9 = (f32[8,1,256]{2,1,0:T(1,128)S(1)}, f32[8,1,256]{2,1,0:T(1,128)S(1)}, u32[]{:S(2)}, u32[]{:S(2)}) collective-permute-start(f32[8,1,256]{2,1,0:T(1,128)S(1)} %get-tuple-element.41), channel_id=1, source_target_pairs={{1,0},{2,1},{3,2},{4,3},{5,4},{6,5},{7,6},{8,7},{9,8},{10,9},{11,1... | collective-permute-start | bytes 24584 | tf_op jit(solution)/shard_map/ppermute | solution.py:18
  105.7 4.5 collective-permute-start.10
  107.9 6.2 collective-permute-start.11
  114.3 4.4 collective-permute-start.12
  116.3 6.2 collective-permute-start.13
  122.7 5.2 collective-permute-start.14
  124.7 6.2 collective-permute-start.15
  131.1 5.3 collective-permute-start.16
  133.1 6.2 collective-permute-start.17
  142.5 346.6 %all-reduce.27.cloned.1.call-start = ((), (), s32[]{:S(2)}) async-start(), calls=%async_computation.4 | async-start | bytes 1048576 | tf_op jit(solution)/shard_map/psum | solution.py:141
  206.3 8.8 %collective-permute-start.18 = (f32[8,1,256]{2,1,0:T(1,128)S(1)}, f32[8,1,256]{2,1,0:T(1,128)S(1)}, u32[]{:S(2)}, u32[]{:S(2)}) collective-permute-start(f32[8,1,256]{2,1,0:T(1,128)S(1)} %get-tuple-element.30), channel_id=1, source_target_pairs={{0,1},{1,2},{2,3},{3,4},{4,5},{5,6},{6,7},{7,8},{8,9},{9,10},{10,1... | collective-permute-start | bytes 24584 | tf_op jit(solution)/shard_map/ppermute | solution.py:15
  213.2 5.0 collective-permute-start.19
  218.4 4.3 collective-permute-start.20
  220.4 5.0 collective-permute-start.21
  225.6 4.3 collective-permute-start.22
  227.6 5.0 collective-permute-start.23
  232.8 5.2 collective-permute-start.24
  234.8 7.2 %collective-permute-start.25 = (f32[8,1,256]{2,1,0:T(1,128)S(1)}, f32[8,1,256]{2,1,0:T(1,128)S(1)}, u32[]{:S(2)}, u32[]{:S(2)}) collective-permute-start(f32[8,1,256]{2,1,0:T(1,128)S(1)} %get-tuple-element.25), channel_id=1, source_target_pairs={{1,0},{2,1},{3,2},{4,3},{5,4},{6,5},{7,6},{8,7},{9,8},{10,9},{11,1... | collective-permute-start | bytes 24584 | tf_op jit(solution)/shard_map/ppermute | solution.py:18
  404.4 6.4 %collective-permute-start.26 = (f32[8,1,256]{2,1,0:T(1,128)S(1)}, f32[8,1,256]{2,1,0:T(1,128)S(1)}, u32[]{:S(2)}, u32[]{:S(2)}) collective-permute-start(f32[8,1,256]{2,1,0:T(1,128)S(1)} %get-tuple-element.22), channel_id=1, source_target_pairs={{0,1},{1,2},{2,3},{3,4},{4,5},{5,6},{6,7},{7,8},{8,9},{9,10},{10,1... | collective-permute-start | bytes 24584 | tf_op jit(solution)/shard_map/ppermute | solution.py:15
  408.7 5.0 collective-permute-start.27
  413.9 4.3 collective-permute-start.28
  415.9 5.0 collective-permute-start.29
  421.1 4.3 collective-permute-start.30
  423.1 5.0 collective-permute-start.31
  428.3 4.3 collective-permute-start.32
  430.3 5.0 collective-permute-start.33
  498.1 8.8 %collective-permute-start.34 = (f32[8,1,256]{2,1,0:T(1,128)S(1)}, f32[8,1,256]{2,1,0:T(1,128)S(1)}, u32[]{:S(2)}, u32[]{:S(2)}) collective-permute-start(f32[8,1,256]{2,1,0:T(1,128)S(1)} %get-tuple-element.14), channel_id=1, source_target_pairs={{0,1},{1,2},{2,3},{3,4},{4,5},{5,6},{6,7},{7,8},{8,9},{9,10},{10,1... | collective-permute-start | bytes 24584 | tf_op jit(solution)/shard_map/ppermute | solution.py:15
  504.9 5.0 collective-permute-start.35
  510.2 4.3 collective-permute-start.36
  512.1 5.0 collective-permute-start.37
  517.4 4.3 collective-permute-start.38
  519.3 5.0 collective-permute-start.39
  524.6 5.2 collective-permute-start.40
  526.5 7.2 %collective-permute-start.41 = (f32[8,1,256]{2,1,0:T(1,128)S(1)}, f32[8,1,256]{2,1,0:T(1,128)S(1)}, u32[]{:S(2)}, u32[]{:S(2)}) collective-permute-start(f32[8,1,256]{2,1,0:T(1,128)S(1)} %get-tuple-element.9), channel_id=1, source_target_pairs={{1,0},{2,1},{3,2},{4,3},{5,4},{6,5},{7,6},{8,7},{9,8},{10,9},{11,1... | collective-permute-start | bytes 24584 | tf_op jit(solution)/shard_map/ppermute | solution.py:18
  (7 other events, 180.4 us)
Sparse Core Ops, SparseCore 0:
  142.7 54.6 all-reduce.24
  440.6 48.5 all-reduce.26
where the time goes:
time: 629 us; the launch traced here: 627 us
  blocking collectives  234 us (37%)
  waiting for transfers between devices  182 us (29%)
  starting transfers between devices  127 us (20%)
  between operations  25.3 us (4%)
  other arithmetic  22.1 us (4%)
  local copies, waits for them, and re-layouts  18.9 us (3%)
  matrix products  17.4 us (3%)
    psum x2, waiting for transfers between devices, shards(): image_part = lax.psum(partial_sum, 'mem')  104 us
    psum x1, blocking collectives, shards(): norm_now = lax.psum(local_inner(residual, residual), ('mem', 'col'))  80.6 us
    psum x1, blocking collectives, shards(): step = norm_now / lax.psum(local_inner(direction, image), ('mem', 'col'))  80.6 us
    psum x1, blocking collectives, shards(): norm_next = lax.psum(local_inner(residual, residual), ('mem', 'col'))  73.2 us
    ppermute x21, waiting for transfers between devices, extended(): lax.ppermute(lax.slice_in_dim(block, 0, width, axis=dim), axis, backward)  64.5 us
    ppermute x21, starting transfers between devices, extended(): lax.ppermute(lax.slice_in_dim(block, block.shape[dim] - width, None, axis...  56 us
    ppermute x21, starting transfers between devices, extended(): lax.ppermute(lax.slice_in_dim(block, 0, width, axis=dim), axis, backward)  47.9 us
    all_to_all x1, starting transfers between devices, shards(): lax.all_to_all(send_cells.reshape(blocks, capacity), 'col', split_axis=0,...  13.1 us
  transfers between devices with their start and end apart: 47, of which 25 were waited for; matrix products, arithmetic and copies ran while one was open for 2% of the time, Pallas kernels for 0%

commit v1 on v0

--- a/solution.py
+++ b/solution.py
@@ -5,6 +5,10 @@
 
 NSWEEP = 4
 ITERS = 2
+
+
+def play_corner(lane_axis, my_data):
+    return jnp.sum(lax.all_gather(my_data, lane_axis), 0)
 
 
 def extended(block, sides, width):
@@ -138,7 +142,7 @@
         ).reshape(rows_here, quarter, features)
         own_slice = lax.dynamic_slice_in_dim(partial_sum, offset, quarter, 1) + forward_static
         partial_sum = lax.dynamic_update_slice_in_dim(partial_sum, own_slice, offset, 1)
-        image_part = lax.psum(partial_sum, "mem")
+        image_part = play_corner("mem", my_data=partial_sum)
         own_image = lax.dynamic_slice_in_dim(image_part, offset, quarter, 1)
         image_part, own_image = (image_part, own_image)
         gathered = image_part.reshape(rows_here * columns, features)[obs_index]

time: 629 us -> 609 us (0.968)
  waiting for transfers between devices: 182 us -> 156 us
  other arithmetic: 22.1 us -> 29.4 us
    psum x2 -> x0, waiting for transfers between devices: 104 us -> none  [shards(): image_part = lax.psum(partial_sum, 'mem')]
    all_gather x0 -> x2, waiting for transfers between devices: none -> 77.5 us  [play_corner(): return jnp.sum(lax.all_gather(my_data, lane_axis), 0)]
where the time goes in v1:
time: 609 us; the launch traced here: 606 us
  blocking collectives  234 us (38%)
  waiting for transfers between devices  156 us (26%)
  starting transfers between devices  122 us (20%)
  other arithmetic  29.4 us (5%)
  between operations  25.2 us (4%)
  matrix products  19.9 us (3%)
  local copies, waits for them, and re-layouts  19.2 us (3%)
    psum x1, blocking collectives, shards(): norm_now = lax.psum(local_inner(residual, residual), ('mem', 'col'))  80.5 us
    psum x1, blocking collectives, shards(): step = norm_now / lax.psum(local_inner(direction, image), ('mem', 'col'))  80.4 us
    all_gather x2, waiting for transfers between devices, play_corner(): return jnp.sum(lax.all_gather(my_data, lane_axis), 0)  77.5 us
    psum x1, blocking collectives, shards(): norm_next = lax.psum(local_inner(residual, residual), ('mem', 'col'))  72.7 us
    ppermute x21, waiting for transfers between devices, extended(): lax.ppermute(lax.slice_in_dim(block, 0, width, axis=dim), axis, backward)  64.4 us
    ppermute x21, starting transfers between devices, extended(): lax.ppermute(lax.slice_in_dim(block, block.shape[dim] - width, None, axis...  51.9 us
    ppermute x21, starting transfers between devices, extended(): lax.ppermute(lax.slice_in_dim(block, 0, width, axis=dim), axis, backward)  47.9 us
    all_to_all x1, starting transfers between devices, shards(): lax.all_to_all(send_cells.reshape(blocks, capacity), 'col', split_axis=0,...  13.1 us
  transfers between devices with their start and end apart: 47, of which 25 were waited for; matrix products, arithmetic and copies ran while one was open for 2% of the time, Pallas kernels for 0%

profile of v1, /device:TPU:1, one launch (start us, length us, event | category | flops | bytes accessed | tf_op | source)
XLA Modules:
  0.0 606.1 jit_solution(3850877065599096292)
XLA Ops:
  13.3 13.1 %all-to-all-start = ((s32[64,1,8]{2,1,0:T(1,128)}), s32[64,1,8]{2,1,0:T(1,128)S(1)}, u32[]{:S(2)}, u32[]{:S(2)}) async-start(s32[64,1,8]{2,1,0:T(1,128)} %bitcast.6), calls=%async_computation | async-start | bytes 65536 | tf_op jit(solution)/shard_map/all_to_all | solution.py:97
  28.5 7.1 %all-to-all-done = s32[64,1,8]{2,1,0:T(1,128)S(1)} async-done(((s32[64,1,8]{2,1,0:T(1,128)}), s32[64,1,8]{2,1,0:T(1,128)S(1)}, u32[]{:S(2)}, u32[]{:S(2)}) %all-to-all-start) | async-done | bytes 2080 | tf_op jit(solution)/shard_map/all_to_all | solution.py:97
  35.7 4.7 all-to-all-start.1
  42.5 7.2 %all-to-all-done.1 = f32[64,1,8]{2,1,0:T(1,128)S(1)} async-done(((f32[64,1,8]{2,1,0:T(1,128)}), f32[64,1,8]{2,1,0:T(1,128)S(1)}, u32[]{:S(2)}, u32[]{:S(2)}) %all-to-all-start.1) | async-done | bytes 2080 | tf_op jit(solution)/shard_map/all_to_all | solution.py:100
  49.7 4.7 all-to-all-start.2
  55.3 3.5 collective-permute-start
  60.7 3.2 collective-permute-done.2
  68.8 2.4 scatter_custom_fusion.3
  73.1 3.3 collective-permute-start.1
  78.4 2.9 collective-permute-done.3
  83.6 2.4 collective-permute-start.5
  86.0 2.6 collective-permute-done.5
  90.8 2.4 collective-permute-start.7
  93.2 2.9 collective-permute-done.7
  98.3 2.4 collective-permute-start.9
  100.7 4.8 collective-permute-done.9
  107.9 2.4 collective-permute-start.11
  110.3 3.8 collective-permute-done.11
  118.7 3.8 collective-permute-done.13
  124.7 2.4 collective-permute-start.15
  128.0 2.9 collective-permute-done.15
  133.1 2.4 collective-permute-start.17
  135.8 3.5 collective-permute-done.17
  142.7 41.9 %all-gather.3.cloned.1.call-done = f32[4,4,256,128]{3,2,1,0:T(8,128)} async-done(((f32[1,4,256,128]{3,2,1,0:T(8,128)}), f32[4,4,256,128]{3,2,1,0:T(8,128)}) %all-gather.3.cloned.1.call-update) | async-done | bytes 2097168 | tf_op jit(solution)/shard_map/all_gather | solution.py:11
  188.9 2.8 scatter_custom_fusion.4
  191.8 2.4 fusion.7
  195.3 4.8 collective-permute-start.18
  202.1 3.0 collective-permute-done.19
  207.4 2.4 collective-permute-start.21
  209.8 2.6 collective-permute-done.21
  217.0 2.6 collective-permute-done.23
  225.1 3.9 collective-permute-done.25
  232.3 80.5 %all-reduce.21 = (f32[]{:T(128)}, f32[]{:T(128)}) all-reduce(f32[]{:T(128)S(6)} %add.397, f32[]{:T(128)S(6)} %add.433), channel_id=1, replica_groups=mesh['mem'=4,'col'=64] {'mem','col'}, use_global_device_ids=true, to_apply=%region_9.10 | all-reduce | flops 2 | bytes 16 | tf_op jit(solution)/shard_map/psum | solution.py:132
  316.8 72.7 %psum.30 = f32[]{:T(128)} all-reduce(f32[]{:T(128)S(6)} %add.434), channel_id=1, replica_groups=mesh['mem'=4,'col'=64] {'mem','col'}, use_global_device_ids=true, to_apply=%region_17.18 | all-reduce | flops 1 | bytes 8 | tf_op jit(solution)/shard_map/psum | solution.py:154
  390.9 4.2 collective-permute-start.26
  397.3 3.0 collective-permute-done.27
  405.0 2.6 collective-permute-done.29
  412.1 2.6 collective-permute-done.31
  419.3 2.6 collective-permute-done.33
  426.9 35.5 %all-gather.5.cloned.1.call-done = f32[4,4,256,128]{3,2,1,0:T(8,128)} async-done(((f32[1,4,256,128]{3,2,1,0:T(8,128)}), f32[4,4,256,128]{3,2,1,0:T(8,128)}) %all-gather.5.cloned.1.call-update) | async-done | bytes 2097168 | tf_op jit(solution)/shard_map/all_gather | solution.py:11
  469.2 3.5 scatter_custom_fusion.5
  473.8 2.4 fusion.3
  478.8 4.8 collective-permute-start.34
  485.5 3.0 collective-permute-done.35
  494.8 2.6 collective-permute-done.37
  502.0 2.6 collective-permute-done.39
  511.0 3.0 collective-permute-done.41
  516.2 80.4 %psum.31 = f32[]{:T(128)} all-reduce(f32[]{:T(128)S(6)} %add.472), channel_id=1, replica_groups=mesh['mem'=4,'col'=64] {'mem','col'}, use_global_device_ids=true, to_apply=%region_22.23 | all-reduce | flops 1 | bytes 8 | tf_op jit(solution)/shard_map/psum | solution.py:152
  (196 shorter events, 117.7 us)
Async XLA Ops:
  13.3 22.4 %all-to-all-start = ((s32[64,1,8]{2,1,0:T(1,128)}), s32[64,1,8]{2,1,0:T(1,128)S(1)}, u32[]{:S(2)}, u32[]{:S(2)}) async-start(s32[64,1,8]{2,1,0:T(1,128)} %bitcast.6), calls=%async_computation | async-start | bytes 65536 | tf_op jit(solution)/shard_map/all_to_all | solution.py:97
  35.7 14.1 %all-to-all-start.1 = ((f32[64,1,8]{2,1,0:T(1,128)}), f32[64,1,8]{2,1,0:T(1,128)S(1)}, u32[]{:S(2)}, u32[]{:S(2)}) async-start(f32[64,1,8]{2,1,0:T(1,128)} %bitcast.8), calls=%async_computation.1 | async-start | bytes 65536 | tf_op jit(solution)/shard_map/all_to_all | solution.py:100
  49.7 17.7 %all-to-all-start.2 = ((f32[64,8,128]{2,1,0:T(8,128)}), f32[64,8,128]{2,1,0:T(8,128)S(1)}, u32[]{:S(2)}, u32[]{:S(2)}) async-start(f32[64,8,128]{2,1,0:T(8,128)} %bitcast.9), calls=%async_computation.2 | async-start | bytes 524288 | tf_op jit(solution)/shard_map/all_to_all | solution.py:90
  54.4 130.2 %all-gather.3.cloned.1.call-start = ((), (), s32[]{:S(2)}) async-start(), calls=%async_computation.3 | async-start | bytes 2621440 | tf_op jit(solution)/shard_map/all_gather | solution.py:11
  55.3 5.5 collective-permute-start
  58.8 5.2 collective-permute-start.2
  67.5 121.4 %copy-start.8 = (s32[512,1]{0,1:T(1,128)}, s32[512,1]{0,1:T(1,128)S(1)}, u32[]{:S(2)}) copy-start(s32[512,1]{0,1:T(1,128)S(1)} %compare_select_fusion) | copy-start | bytes 6148
  73.1 5.3 collective-permute-start.1
  76.4 5.0 collective-permute-start.3
  81.6 4.3 collective-permute-start.4
  83.6 5.0 collective-permute-start.5
  88.8 4.3 collective-permute-start.6
  90.8 5.3 collective-permute-start.7
  96.3 4.3 collective-permute-start.8
  98.3 7.2 %collective-permute-start.9 = (f32[8,1,256]{2,1,0:T(1,128)S(1)}, f32[8,1,256]{2,1,0:T(1,128)S(1)}, u32[]{:S(2)}, u32[]{:S(2)}) collective-permute-start(f32[8,1,256]{2,1,0:T(1,128)S(1)} %get-tuple-element.41), channel_id=1, source_target_pairs={{1,0},{2,1},{3,2},{4,3},{5,4},{6,5},{7,6},{8,7},{9,8},{10,9},{11,1... | collective-permute-start | bytes 24584 | tf_op jit(solution)/shard_map/ppermute | solution.py:22
  105.8 4.5 collective-permute-start.10
  107.9 6.2 %collective-permute-start.11 = (f32[8,1,256]{2,1,0:T(1,128)S(1)}, f32[8,1,256]{2,1,0:T(1,128)S(1)}, u32[]{:S(2)}, u32[]{:S(2)}) collective-permute-start(f32[8,1,256]{2,1,0:T(1,128)S(1)} %get-tuple-element.39), channel_id=1, source_target_pairs={{1,0},{2,1},{3,2},{4,3},{5,4},{6,5},{7,6},{8,7},{9,8},{10,9},{11,1... | collective-permute-start | bytes 24584 | tf_op jit(solution)/shard_map/ppermute | solution.py:22
  114.3 4.4 collective-permute-start.12
  116.3 6.2 %collective-permute-start.13 = (f32[8,1,256]{2,1,0:T(1,128)S(1)}, f32[8,1,256]{2,1,0:T(1,128)S(1)}, u32[]{:S(2)}, u32[]{:S(2)}) collective-permute-start(f32[8,1,256]{2,1,0:T(1,128)S(1)} %get-tuple-element.37), channel_id=1, source_target_pairs={{1,0},{2,1},{3,2},{4,3},{5,4},{6,5},{7,6},{8,7},{9,8},{10,9},{11,1... | collective-permute-start | bytes 24584 | tf_op jit(solution)/shard_map/ppermute | solution.py:22
  122.7 5.2 collective-permute-start.14
  124.7 6.2 %collective-permute-start.15 = (f32[8,1,256]{2,1,0:T(1,128)S(1)}, f32[8,1,256]{2,1,0:T(1,128)S(1)}, u32[]{:S(2)}, u32[]{:S(2)}) collective-permute-start(f32[8,1,256]{2,1,0:T(1,128)S(1)} %get-tuple-element.35), channel_id=1, source_target_pairs={{1,0},{2,1},{3,2},{4,3},{5,4},{6,5},{7,6},{8,7},{9,8},{10,9},{11,1... | collective-permute-start | bytes 24584 | tf_op jit(solution)/shard_map/ppermute | solution.py:22
  131.1 4.6 collective-permute-start.16
  133.1 6.2 %collective-permute-start.17 = (f32[8,1,256]{2,1,0:T(1,128)S(1)}, f32[8,1,256]{2,1,0:T(1,128)S(1)}, u32[]{:S(2)}, u32[]{:S(2)}) collective-permute-start(f32[8,1,256]{2,1,0:T(1,128)S(1)} %get-tuple-element.33), channel_id=1, source_target_pairs={{1,0},{2,1},{3,2},{4,3},{5,4},{6,5},{7,6},{8,7},{9,8},{10,9},{11,1... | collective-permute-start | bytes 24584 | tf_op jit(solution)/shard_map/ppermute | solution.py:22
  142.6 319.8 %all-gather.5.cloned.1.call-start = ((), (), s32[]{:S(2)}) async-start(), calls=%async_computation.4 | async-start | bytes 2621440 | tf_op jit(solution)/shard_map/all_gather | solution.py:11
  195.3 6.8 %collective-permute-start.18 = (f32[8,1,256]{2,1,0:T(1,128)S(1)}, f32[8,1,256]{2,1,0:T(1,128)S(1)}, u32[]{:S(2)}, u32[]{:S(2)}) collective-permute-start(f32[8,1,256]{2,1,0:T(1,128)S(1)} %get-tuple-element.30), channel_id=1, source_target_pairs={{0,1},{1,2},{2,3},{3,4},{4,5},{5,6},{6,7},{7,8},{8,9},{9,10},{10,1... | collective-permute-start | bytes 24584 | tf_op jit(solution)/shard_map/ppermute | solution.py:19
  200.2 5.0 collective-permute-start.19
  205.4 4.3 collective-permute-start.20
  207.4 5.0 collective-permute-start.21
  212.6 4.3 collective-permute-start.22
  214.6 5.0 collective-permute-start.23
  219.8 5.3 collective-permute-start.24
  221.7 7.2 %collective-permute-start.25 = (f32[8,1,256]{2,1,0:T(1,128)S(1)}, f32[8,1,256]{2,1,0:T(1,128)S(1)}, u32[]{:S(2)}, u32[]{:S(2)}) collective-permute-start(f32[8,1,256]{2,1,0:T(1,128)S(1)} %get-tuple-element.25), channel_id=1, source_target_pairs={{1,0},{2,1},{3,2},{4,3},{5,4},{6,5},{7,6},{8,7},{9,8},{10,9},{11,1... | collective-permute-start | bytes 24584 | tf_op jit(solution)/shard_map/ppermute | solution.py:22
  390.9 6.4 %collective-permute-start.26 = (f32[8,1,256]{2,1,0:T(1,128)S(1)}, f32[8,1,256]{2,1,0:T(1,128)S(1)}, u32[]{:S(2)}, u32[]{:S(2)}) collective-permute-start(f32[8,1,256]{2,1,0:T(1,128)S(1)} %get-tuple-element.22), channel_id=1, source_target_pairs={{0,1},{1,2},{2,3},{3,4},{4,5},{5,6},{6,7},{7,8},{8,9},{9,10},{10,1... | collective-permute-start | bytes 24584 | tf_op jit(solution)/shard_map/ppermute | solution.py:19
  395.1 5.2 collective-permute-start.27
  400.6 4.3 collective-permute-start.28
  402.6 5.0 collective-permute-start.29
  407.8 4.3 collective-permute-start.30
  409.8 5.0 collective-permute-start.31
  415.0 4.3 collective-permute-start.32
  416.9 5.0 collective-permute-start.33
  478.8 6.8 %collective-permute-start.34 = (f32[8,1,256]{2,1,0:T(1,128)S(1)}, f32[8,1,256]{2,1,0:T(1,128)S(1)}, u32[]{:S(2)}, u32[]{:S(2)}) collective-permute-start(f32[8,1,256]{2,1,0:T(1,128)S(1)} %get-tuple-element.14), channel_id=1, source_target_pairs={{0,1},{1,2},{2,3},{3,4},{4,5},{5,6},{6,7},{7,8},{8,9},{9,10},{10,1... | collective-permute-start | bytes 24584 | tf_op jit(solution)/shard_map/ppermute | solution.py:19
  483.6 5.0 collective-permute-start.35
  490.5 4.3 collective-permute-start.36
  492.4 5.0 collective-permute-start.37
  497.7 4.3 collective-permute-start.38
  499.6 5.0 collective-permute-start.39
  504.9 6.1 %collective-permute-start.40 = (f32[8,1,256]{2,1,0:T(1,128)S(1)}, f32[8,1,256]{2,1,0:T(1,128)S(1)}, u32[]{:S(2)}, u32[]{:S(2)}) collective-permute-start(f32[8,1,256]{2,1,0:T(1,128)S(1)} %get-tuple-element.8), channel_id=1, source_target_pairs={{0,1},{1,2},{2,3},{3,4},{4,5},{5,6},{6,7},{7,8},{8,9},{9,10},{10,1... | collective-permute-start | bytes 24584 | tf_op jit(solution)/shard_map/ppermute | solution.py:19
  506.8 7.2 %collective-permute-start.41 = (f32[8,1,256]{2,1,0:T(1,128)S(1)}, f32[8,1,256]{2,1,0:T(1,128)S(1)}, u32[]{:S(2)}, u32[]{:S(2)}) collective-permute-start(f32[8,1,256]{2,1,0:T(1,128)S(1)} %get-tuple-element.9), channel_id=1, source_target_pairs={{1,0},{2,1},{3,2},{4,3},{5,4},{6,5},{7,6},{8,7},{9,8},{10,9},{11,1... | collective-permute-start | bytes 24584 | tf_op jit(solution)/shard_map/ppermute | solution.py:22
  (9 other events, 381.4 us)
Sparse Core Ops, SparseCore 0:
  142.7 41.8 all-gather.2
  427.0 35.3 all-gather.4
